TPU v7x, 512 devices: a whole 4x4x16 slice. The times are simulated.
512 devices in a mesh: seq: 64 (over z, y), tensor: 8 (over x, core).
Axes of the slice: x: 4, y: 4, z: 16, core: 2. Of those that a mesh axis runs over, the one named last changes fastest.
Arguments:
- hidden: bfloat16 [8192, 4096], P('seq', 'tensor')
- norm_gain: bfloat16 [4096], replicated, may hold values from 0.5 to 1.5
- w_query: bfloat16 [4096, 4096], P('seq', 'tensor')
- key_value_weight: bfloat16 [4096, 1024], P('seq')
- w_out: bfloat16 [4096, 4096], P('tensor', 'seq'), may hold values from -0.09375 to 0.09375
- prefix_key_cache: bfloat16 [64, 1024, 1024], P('seq')
- prefix_owner: int32 [64], replicated, may hold values from 0 to 63, each once
- token_counts: int32 [64, 64], P('seq'), may hold values from 0 to 4, as said below
Outputs:
- attn_out: bfloat16 [8192, 4096], P('seq', 'tensor')
- suffix_key_cache: bfloat16 [8192, 1024], P('seq', 'tensor')
Inputs may be any that keep to these rules, and one draw needn't show every extreme that they name: `token_counts`: each row sums to 128; one prefix receives exactly 4 tokens from every sequence index.
All inputs are finite; a program needn't handle non-finite values.
Results may differ from a plain program's by a relative error of at most 0.035.
Values may be sent and summed in bfloat16 or wider, within the bound.
No kernel may reach another device: no remote copies, remote signals or barrier semaphores. Data moves between devices by JAX's collectives and lax.ppermute only.
A program may use at most 64 MiB of HBM per device.

v0:
```python
import jax
import jax.numpy as jnp
from jax import lax
from jax.sharding import PartitionSpec as P

HEAD_DIM = 128
PREFIX_LENGTH = 1024
eps = 1e-06
theta = 5000000.0


def rotate(values, positions):
    half = values.shape[-1] // 2
    frequency = theta ** (-jnp.arange(half, dtype=jnp.float32) * 2.0 / values.shape[-1])
    angle = positions.astype(jnp.float32)[:, None] * frequency[None, :]
    cosine = jnp.cos(angle)[:, None, :]
    sine = jnp.sin(angle)[:, None, :]
    first = values[..., :half]
    second = values[..., half:]
    return jnp.concatenate(
        [first * cosine - second * sine, second * cosine + first * sine], axis=-1
    )


def layout(counts_row, length):
    ends = jnp.cumsum(counts_row)
    starts = ends - counts_row
    places = jnp.arange(length, dtype=jnp.int32)
    member = (places[:, None] >= starts[None, :]) & (places[:, None] < ends[None, :])
    labels = jnp.arange(counts_row.shape[0], dtype=jnp.int32)
    prefix_group = jnp.sum(jnp.where(member, labels[None, :], 0), axis=1)
    offset = places - jnp.sum(jnp.where(member, starts[None, :], 0), axis=1)
    return (starts, prefix_group, offset)


def attend(query_vectors, keys, values, allowed):
    scores = lax.dot_general(
        query_vectors, keys, (((1,), (1,)), ((), ())), preferred_element_type=jnp.float32
    )
    scores = scores * (1.0 / query_vectors.shape[-1] ** 0.5)
    if allowed is not None:
        scores = jnp.where(allowed, scores, -1e30)
    top = jnp.max(scores, axis=1, keepdims=True)
    expo = jnp.exp(scores - top)
    total = jnp.sum(expo, axis=1, keepdims=True)
    weights = (expo / total).astype(jnp.bfloat16)
    result = jnp.dot(weights, values, preferred_element_type=jnp.float32)
    return (result, top[:, 0] + jnp.log(total[:, 0]))


def shards(
    hidden,
    norm_gain,
    w_query,
    key_value_weight,
    w_out,
    prefix_key_cache,
    prefix_owner,
    token_counts,
):
    tensor_index = lax.axis_index("tensor")
    tensor_count = lax.axis_size("tensor")
    seq_count = lax.axis_size("seq")
    length = hidden.shape[0]
    head_size = HEAD_DIM
    whole = lax.all_gather(hidden, "tensor", axis=1, tiled=True)
    wide = whole.astype(jnp.float32)
    normalized_input = (
        wide
        * lax.rsqrt(jnp.mean(wide * wide, axis=1, keepdims=True) + eps)
        * norm_gain.astype(jnp.float32)
    ).astype(jnp.bfloat16)
    width_query = w_query.shape[1]
    full_width = key_value_weight.shape[1]
    heads_dev = width_query // head_size
    kv_heads = full_width // (2 * head_size)

    def contract(piece):
        return jnp.dot(normalized_input, piece, preferred_element_type=jnp.float32)

    query_vectors = contract(lax.all_gather(w_query, "seq", axis=0, tiled=True))
    key_value_pair = contract(lax.all_gather(key_value_weight, "seq", axis=0, tiled=True))
    counts = token_counts[0]
    num_groups = counts.shape[0]
    starts, prefix_group, offset = layout(counts, length)
    positions = PREFIX_LENGTH + offset
    query_vectors = rotate(query_vectors.reshape(length, heads_dev, head_size), positions).astype(
        jnp.bfloat16
    )
    pair_blocks = key_value_pair.reshape(length, kv_heads, 2, head_size)
    rotated_keys = rotate(pair_blocks[:, :, 0], positions)
    pair_all = jnp.stack([rotated_keys, pair_blocks[:, :, 1]], axis=2).astype(jnp.bfloat16)
    suffix_full = pair_all.reshape(length, full_width)
    share = full_width // tensor_count
    suffix_part = lax.dynamic_slice_in_dim(suffix_full, tensor_index * share, share, 1)
    group_full = heads_dev * tensor_count // kv_heads
    kv_local = max(1, heads_dev // group_full)
    kv_start = tensor_index * heads_dev // group_full
    suffix_mine = lax.dynamic_slice_in_dim(pair_all, kv_start, kv_local, 1)
    suffix_keys = suffix_mine[:, :, 0]
    suffix_values = suffix_mine[:, :, 1]
    cache_all = prefix_key_cache[0].reshape(-1, kv_heads, 2, head_size)
    cache_mine = lax.dynamic_slice_in_dim(cache_all, kv_start, kv_local, 1)
    cache_keys = cache_mine[:, :, 0]
    cache_values = cache_mine[:, :, 1]
    group_width = heads_dev // kv_local
    capacity = 2 * length // seq_count
    labels = jnp.arange(num_groups, dtype=jnp.int32)
    owner_match = prefix_owner[None, :] == jnp.arange(seq_count, dtype=jnp.int32)[:, None]
    owner_start = jnp.sum(jnp.where(owner_match, starts[None, :], 0), axis=1)
    owner_count = jnp.sum(jnp.where(owner_match, counts[None, :], 0), axis=1)
    slots = jnp.arange(capacity, dtype=jnp.int32)
    valid = slots[None, :] < owner_count[:, None]
    source_rows = jnp.where(valid, owner_start[:, None] + slots[None, :], 0)
    flat_query = query_vectors.reshape(length, width_query)
    outgoing = jnp.where(valid[:, :, None], flat_query[source_rows], jnp.zeros((), jnp.bfloat16))
    arrived = lax.all_to_all(outgoing, "seq", split_axis=0, concat_axis=0, tiled=True)
    items = arrived.shape[1]
    rows_in = arrived.reshape(seq_count * items, heads_dev, head_size)
    outs = []
    logs = []
    for serve_head in range(heads_dev):
        serve_result, serve_logsum = attend(
            rows_in[:, serve_head],
            cache_keys[:, serve_head // group_width],
            cache_values[:, serve_head // group_width],
            None,
        )
        outs.append(serve_result)
        logs.append(serve_logsum)
    out_block = jnp.stack(outs, axis=1).astype(jnp.bfloat16).reshape(seq_count, items, width_query)
    log_block = jnp.stack(logs, axis=1).reshape(seq_count, items, heads_dev)
    prefix_out = lax.all_to_all(out_block, "seq", split_axis=0, concat_axis=0, tiled=True)
    prefix_log = lax.all_to_all(
        log_block.astype(jnp.bfloat16), "seq", split_axis=0, concat_axis=0, tiled=True
    ).astype(log_block.dtype)
    owner_of_token = jnp.sum(
        jnp.where(prefix_group[:, None] == labels[None, :], prefix_owner[None, :], 0), axis=1
    )
    back_rows = owner_of_token * capacity + offset
    prefix_rows = prefix_out.reshape(seq_count * capacity, heads_dev, head_size)[back_rows]
    prefix_logsum = prefix_log.reshape(seq_count * capacity, heads_dev)[back_rows]
    places = jnp.arange(length, dtype=jnp.int32)
    allowed = (prefix_group[:, None] == prefix_group[None, :]) & (
        places[None, :] <= places[:, None]
    )
    outs = []
    logs = []
    for head in range(heads_dev):
        result, logsum = attend(
            query_vectors[:, head],
            suffix_keys[:, head // group_width],
            suffix_values[:, head // group_width],
            allowed,
        )
        outs.append(result)
        logs.append(logsum)
    suffix_attn = jnp.stack(outs, axis=1)
    suffix_logsum = jnp.stack(logs, axis=1)
    upper = jnp.maximum(prefix_logsum, suffix_logsum)
    left = jnp.exp(prefix_logsum - upper)[..., None]
    right = jnp.exp(suffix_logsum - upper)[..., None]
    context = (
        (left * prefix_rows.astype(jnp.float32) + right * suffix_attn) / (left + right)
    ).astype(jnp.bfloat16)
    context = context.reshape(length, width_query)
    partial_out = jnp.dot(
        context,
        lax.all_gather(w_out, "seq", axis=1, tiled=True),
        preferred_element_type=jnp.float32,
    )
    attn_out = lax.psum_scatter(
        partial_out.astype(jnp.bfloat16), "tensor", scatter_dimension=1, tiled=True
    )
    return (attn_out, suffix_part)


def solution(mesh):
    in_specs = (
        P("seq", "tensor"),
        P(),
        P("seq", "tensor"),
        P("seq", None),
        P("tensor", "seq"),
        P("seq", None, None),
        P(),
        P("seq", None),
    )
    out_specs = (P("seq", "tensor"), P("seq", "tensor"))
    return jax.shard_map(shards, mesh=mesh, in_specs=in_specs, out_specs=out_specs, check_vma=False)
```

profile of v0, /device:TPU:8, one launch (start us, length us, event | category | flops | bytes accessed | tf_op | source)
XLA Modules:
  0.0 541.2 jit_solution(3711993992200430537)
XLA Ops:
  7.2 0.7 all-gather.5.cloned.1.call-update
  7.9 0.7 all-gather.7.cloned.1.call-update
  8.7 0.7 all-gather.9.cloned.1.call-update
  10.0 0.7 convert_element_type.73
  10.7 0.7 copy.120
  11.6 0.7 fusion.63
  12.4 2.9 copy.123
  16.5 1.0 multiply_cosine_fusion
  17.4 28.1 %all-gather.5.cloned.1.call-done = bf16[128,4096]{1,0:T(8,128)(2,1)} async-done(((bf16[128,512]{1,0:T(8,128)(2,1)}), bf16[128,4096]{1,0:T(8,128)(2,1)}) %all-gather.5.cloned.1.call-update) | async-done | bytes 1048592 | tf_op jit(solution)/shard_map/all_gather | solution.py:66
  45.6 1.5 fusion
  47.1 146.7 %all-gather.7.cloned.1.call-done = bf16[4096,512]{1,0:T(8,128)(2,1)} async-done(((bf16[64,512]{1,0:T(8,128)(2,1)}), bf16[4096,512]{1,0:T(8,128)(2,1)}) %all-gather.7.cloned.1.call-update) | async-done | bytes 4194320 | tf_op jit(solution)/shard_map/all_gather | solution.py:81
  193.8 4.0 fusion.17
  197.8 1.0 reshape.549
  198.8 0.9 fusion.69
  199.7 148.7 %all-gather.9.cloned.1.call-done = bf16[4096,1024]{1,0:T(8,128)(2,1)} async-done(((bf16[64,1024]{1,0:T(8,128)(2,1)}), bf16[4096,1024]{1,0:T(8,128)(2,1)}) %all-gather.9.cloned.1.call-update) | async-done | bytes 8388624 | tf_op jit(solution)/shard_map/all_gather | solution.py:82
  348.5 5.5 %fusion.15 = f32[128,1024]{1,0:T(8,128)} fusion(bf16[4096,1024]{1,0:T(8,128)(2,1)} %all-gather.9.cloned.1.call-done, bf16[128,4096]{1,0:T(8,128)(2,1)S(1)} %copy-done, f32[4096]{0:T(1024)S(1)} %convert_element_type.73, f32[128]{0:T(128)S(1)} %add_rsqrt_fusion), kind=kOutput, calls=%fused_computation.46 | convolution fusion | flops 1075838976 | bytes 9978368 | tf_op jit(solution)/shard_map/dot_general | solution.py:79
  354.0 1.5 reshape.555
  356.1 1.1 multiply_subtract_fusion
  357.3 1.2 gather_fusion
  358.5 0.9 broadcast_select_fusion
  359.4 10.4 %all-to-all-start = ((bf16[64,4,512]{2,1,0:T(4,128)(2,1)}), bf16[64,4,512]{2,1,0:T(4,128)(2,1)S(1)}, u32[]{:S(2)}, u32[]{:S(2)}) async-start(bf16[64,4,512]{2,1,0:T(4,128)(2,1)} %broadcast_select_fusion), calls=%async_computation | async-start | bytes 524288 | tf_op jit(solution)/shard_map/all_to_all | solution.py:117
  373.2 0.8 convolution_bitcast_fusion
  374.0 14.2 %all-to-all-done = bf16[64,4,512]{2,1,0:T(4,128)(2,1)S(1)} async-done(((bf16[64,4,512]{2,1,0:T(4,128)(2,1)}), bf16[64,4,512]{2,1,0:T(4,128)(2,1)S(1)}, u32[]{:S(2)}, u32[]{:S(2)}) %all-to-all-start) | async-done | bytes 262176 | tf_op jit(solution)/shard_map/all_to_all | solution.py:117
  388.3 1.1 fusion.68
  391.3 0.8 add.239
  392.1 1.3 fusion.75
  393.4 1.0 copy-done.1
  395.7 1.4 add.237
  397.1 1.3 fusion.76
  398.4 1.0 copy-done.3
  400.9 1.4 add.235
  402.6 1.0 copy-done.5
  404.1 0.8 pad_maximum_fusion.1
  404.8 0.7 copy.125
  405.5 5.5 %all-to-all-start.1 = ((bf16[64,4,4]{1,2,0:T(4,128)(2,1)}), bf16[64,4,4]{1,2,0:T(4,128)(2,1)S(1)}, u32[]{:S(2)}, u32[]{:S(2)}) async-start(bf16[64,4,4]{1,2,0:T(4,128)(2,1)} %copy.125), calls=%async_computation.1 | async-start | bytes 131072 | tf_op jit(solution)/shard_map/all_to_all | solution.py:134
  411.1 1.1 fusion.6
  412.7 0.8 copy-done.4
  413.9 0.8 copy-done.6
  415.5 0.8 convert_element_type.83
  416.3 9.3 %all-to-all-done.1 = bf16[64,4,4]{1,2,0:T(4,128)(2,1)S(1)} async-done(((bf16[64,4,4]{1,2,0:T(4,128)(2,1)}), bf16[64,4,4]{1,2,0:T(4,128)(2,1)S(1)}, u32[]{:S(2)}, u32[]{:S(2)}) %all-to-all-start.1) | async-done | bytes 2080 | tf_op jit(solution)/shard_map/all_to_all | solution.py:134
  425.6 5.9 %all-to-all-start.2 = ((bf16[64,4,512]{2,1,0:T(4,128)(2,1)}), bf16[64,4,512]{2,1,0:T(4,128)(2,1)S(1)}, u32[]{:S(2)}, u32[]{:S(2)}) async-start(bf16[64,4,512]{2,1,0:T(4,128)(2,1)} %convert_element_type.83), calls=%async_computation.2 | async-start | bytes 524288 | tf_op jit(solution)/shard_map/all_to_all | solution.py:133
  432.6 0.8 gather_fusion.1
  433.5 16.1 %all-to-all-done.2 = bf16[64,4,512]{2,1,0:T(4,128)(2,1)S(1)} async-done(((bf16[64,4,512]{2,1,0:T(4,128)(2,1)}), bf16[64,4,512]{2,1,0:T(4,128)(2,1)S(1)}, u32[]{:S(2)}, u32[]{:S(2)}) %all-to-all-start.2) | async-done | bytes 262176 | tf_op jit(solution)/shard_map/all_to_all | solution.py:133
  449.7 0.9 gather_fusion.2
  450.8 44.6 %all-gather.11.cloned.1.call-done = bf16[512,4096]{0,1:T(8,128)(2,1)} async-done(((bf16[512,64]{0,1:T(8,128)(2,1)}), bf16[512,4096]{0,1:T(8,128)(2,1)}) %all-gather.11.cloned.1.call-update) | async-done | bytes 4194320 | tf_op jit(solution)/shard_map/all_gather | solution.py:169
  495.3 4.7 convolution_convert_fusion
  500.2 0.7 copy.137
  500.9 33.8 %reduce-scatter.2.cloned.1.call-done = bf16[128,512]{1,0:T(8,128)(2,1)} async-done(((bf16[128,4096]{1,0:T(8,128)(2,1)}), bf16[128,512]{1,0:T(8,128)(2,1)}) %reduce-scatter.2.cloned.1.call-update) | async-done | bytes 131088 | tf_op jit(solution)/shard_map/reduce_scatter | solution.py:172
  (150 shorter events, 14.9 us)
Async XLA Ops:
  7.2 38.4 %all-gather.5.cloned.1.call-start = ((), (), s32[]{:S(2)}) async-start(), calls=%async_computation.4 | async-start | bytes 1179648 | tf_op jit(solution)/shard_map/all_gather | solution.py:66
  7.9 185.9 %all-gather.7.cloned.1.call-start = ((), (), s32[]{:S(2)}) async-start(), calls=%async_computation.5 | async-start | bytes 4259840 | tf_op jit(solution)/shard_map/all_gather | solution.py:81
  8.6 339.8 %all-gather.9.cloned.1.call-start = ((), (), s32[]{:S(2)}) async-start(), calls=%async_computation.6 | async-start | bytes 8519680 | tf_op jit(solution)/shard_map/all_gather | solution.py:82
  9.4 486.0 %all-gather.11.cloned.1.call-start = ((), (), s32[]{:S(2)}) async-start(), calls=%async_computation.7 | async-start | bytes 4259840 | tf_op jit(solution)/shard_map/all_gather | solution.py:169
  12.4 2.9 copy-start.28
  12.4 2.9 copy-start.42
  47.1 301.4 %copy-start = (bf16[128,4096]{1,0:T(8,128)(2,1)S(1)}, bf16[128,4096]{1,0:T(8,128)(2,1)}, u32[]{:S(2)}) copy-start(bf16[128,4096]{1,0:T(8,128)(2,1)} %all-gather.5.cloned.1.call-done) | copy-start | bytes 3145732
  354.0 2.1 copy-start.7
  354.0 2.1 copy-start.8
  359.4 28.7 %all-to-all-start = ((bf16[64,4,512]{2,1,0:T(4,128)(2,1)}), bf16[64,4,512]{2,1,0:T(4,128)(2,1)S(1)}, u32[]{:S(2)}, u32[]{:S(2)}) async-start(bf16[64,4,512]{2,1,0:T(4,128)(2,1)} %broadcast_select_fusion), calls=%async_computation | async-start | bytes 524288 | tf_op jit(solution)/shard_map/all_to_all | solution.py:117
  370.1 3.9 copy-start.29
  370.3 0.9 copy-start.31
  370.3 19.0 %copy-start.9 = (f32[128,128]{0,1:T(8,128)}, f32[128,128]{0,1:T(8,128)S(1)}, u32[]{:S(2)}) copy-start(f32[128,128]{0,1:T(8,128)S(1)} %get-tuple-element.36) | copy-start | bytes 196612
  370.4 3.6 copy-start.33
  371.2 0.6 copy-start.35
  371.2 18.2 %copy-start.11 = (f32[128,128]{0,1:T(8,128)}, f32[128,128]{0,1:T(8,128)S(1)}, u32[]{:S(2)}) copy-start(f32[128,128]{0,1:T(8,128)S(1)} %get-tuple-element.38) | copy-start | bytes 196612
  372.5 1.5 copy-start.13
  372.5 1.5 copy-start.39
  393.4 1.0 copy-start.1
  393.4 1.3 copy-start.17
  398.3 1.0 copy-start.3
  398.3 1.3 copy-start.19
  399.7 0.6 copy-start.26
  402.6 1.0 copy-start.5
  402.6 1.3 copy-start.21
  405.5 20.1 %all-to-all-start.1 = ((bf16[64,4,4]{1,2,0:T(4,128)(2,1)}), bf16[64,4,4]{1,2,0:T(4,128)(2,1)S(1)}, u32[]{:S(2)}, u32[]{:S(2)}) async-start(bf16[64,4,4]{1,2,0:T(4,128)(2,1)} %copy.125), calls=%async_computation.1 | async-start | bytes 131072 | tf_op jit(solution)/shard_map/all_to_all | solution.py:134
  411.1 1.2 copy-start.2
  411.1 1.2 copy-start.18
  411.1 1.2 copy-start.25
  412.3 1.2 copy-start.4
  412.3 1.2 copy-start.20
  412.3 1.2 copy-start.27
  413.5 1.2 copy-start.6
  413.5 1.2 copy-start.22
  415.1 16.4 %copy-start.10 = (f32[128,128]{0,1:T(8,128)S(1)}, f32[128,128]{0,1:T(8,128)}, u32[]{:S(2)}) copy-start(f32[128,128]{0,1:T(8,128)} %copy-done.9) | copy-start | bytes 196612
  415.2 16.4 %copy-start.32 = (f32[128]{0:T(128)S(1)}, f32[128]{0:T(128)}, u32[]{:S(2)}) copy-start(f32[128]{0:T(128)} %copy-done.31) | copy-start | bytes 1540
  415.2 16.4 %copy-start.37 = (f32[128]{0:T(128)S(1)}, f32[128]{0:T(128)}, u32[]{:S(2)}) copy-start(f32[128]{0:T(128)} %fusion.33) | copy-start | bytes 1540
  415.2 16.6 %copy-start.12 = (f32[128,128]{0,1:T(8,128)S(1)}, f32[128,128]{0,1:T(8,128)}, u32[]{:S(2)}) copy-start(f32[128,128]{0,1:T(8,128)} %copy-done.11) | copy-start | bytes 196612
  415.2 16.6 %copy-start.36 = (f32[128]{0:T(128)S(1)}, f32[128]{0:T(128)}, u32[]{:S(2)}) copy-start(f32[128]{0:T(128)} %copy-done.35) | copy-start | bytes 1540
  415.2 16.6 %copy-start.38 = (f32[128]{0:T(128)S(1)}, f32[128]{0:T(128)}, u32[]{:S(2)}) copy-start(f32[128]{0:T(128)} %fusion.32) | copy-start | bytes 1540
  415.2 16.8 %copy-start.14 = (f32[128,128]{0,1:T(8,128)S(1)}, f32[128,128]{0,1:T(8,128)}, u32[]{:S(2)}) copy-start(f32[128,128]{0,1:T(8,128)} %copy-done.13) | copy-start | bytes 196612
  415.2 16.8 %copy-start.40 = (f32[128]{0:T(128)S(1)}, f32[128]{0:T(128)}, u32[]{:S(2)}) copy-start(f32[128]{0:T(128)} %copy-done.39) | copy-start | bytes 1540
  415.2 16.8 %copy-start.41 = (f32[128]{0:T(128)S(1)}, f32[128]{0:T(128)}, u32[]{:S(2)}) copy-start(f32[128]{0:T(128)} %fusion.31) | copy-start | bytes 1540
  415.2 17.1 %copy-start.30 = (f32[128]{0:T(128)S(1)}, f32[128]{0:T(128)}, u32[]{:S(2)}) copy-start(f32[128]{0:T(128)} %copy-done.29) | copy-start | bytes 1540
  415.2 17.1 %copy-start.34 = (f32[128]{0:T(128)S(1)}, f32[128]{0:T(128)}, u32[]{:S(2)}) copy-start(f32[128]{0:T(128)} %copy-done.33) | copy-start | bytes 1540
  415.3 35.4 %copy-start.15 = (f32[128,1,128]{0,2,1:T(8,128)S(1)}, f32[128,1,128]{0,2,1:T(8,128)}, u32[]{:S(2)}) copy-start(f32[128,1,128]{0,2,1:T(8,128)} %convolution_bitcast_fusion) | copy-start | bytes 196612
  425.6 24.0 %all-to-all-start.2 = ((bf16[64,4,512]{2,1,0:T(4,128)(2,1)}), bf16[64,4,512]{2,1,0:T(4,128)(2,1)S(1)}, u32[]{:S(2)}, u32[]{:S(2)}) async-start(bf16[64,4,512]{2,1,0:T(4,128)(2,1)} %convert_element_type.83), calls=%async_computation.2 | async-start | bytes 524288 | tf_op jit(solution)/shard_map/all_to_all | solution.py:133
  431.5 103.2 %reduce-scatter.2.cloned.1.call-start = ((), (), s32[]{:S(2)}) async-start(), calls=%async_computation.8 | async-start | bytes 1179648 | tf_op jit(solution)/shard_map/reduce_scatter | solution.py:172
  (3 other events, 1.6 us)
Sparse Core Ops, SparseCore 0:
  10.1 35.3 all-gather.4
  48.5 145.2 all-gather.6
  196.7 151.7 all-gather.8
  351.3 144.0 all-gather.10
  500.1 34.5 reduce-scatter.1
where the time goes:
time: 542 us; the launch traced here: 541 us
  waiting for transfers between devices  444 us (82%)
  local copies, waits for them, and re-layouts  25.9 us (5%)
  starting transfers between devices  22 us (4%)
  matrix products  21.8 us (4%)
  between operations  14.5 us (3%)
  other arithmetic  13 us (2%)
    all_gather x1, waiting for transfers between devices, shards(): lax.all_gather(key_value_weight, 'seq', axis=0, tiled=True)  149 us
    all_gather x1, waiting for transfers between devices, shards(): query_vectors = contract(lax.all_gather(w_query, 'seq', axis=0, tiled=True))  147 us
    all_gather x1, waiting for transfers between devices, shards(): lax.all_gather(w_out, 'seq', axis=1, tiled=True)  44.6 us
    reduce_scatter x1, waiting for transfers between devices, shards(): lax.psum_scatter(partial_out.astype(jnp.bfloat16), 'tensor', scatter_dime...  33.8 us
    all_gather x1, waiting for transfers between devices, shards(): whole = lax.all_gather(hidden, 'tensor', axis=1, tiled=True)  28.1 us
    all_to_all x1, waiting for transfers between devices, shards(): lax.all_to_all(out_block, 'seq', split_axis=0, concat_axis=0, tiled=True)  16.1 us
    all_to_all x1, waiting for transfers between devices, shards(): lax.all_to_all(outgoing, 'seq', split_axis=0, concat_axis=0, tiled=True)  14.2 us
    unnamed x90, local copies, waits for them, and re-layouts  10.9 us
  transfers between devices with their start and end apart: 8, of which 8 were waited for; matrix products, arithmetic and copies ran while one was open for 9% of the time, Pallas kernels for 0%

commit v1 on v0

--- a/solution.py
+++ b/solution.py
@@ -7,6 +7,12 @@
 PREFIX_LENGTH = 1024
 eps = 1e-06
 theta = 5000000.0
+
+
+def open_shelves_up(view, axis_k):
+    y2 = jnp.concatenate([view for _ in range(lax.axis_size("seq"))], axis_k)
+    block_now = lax.all_to_all(y2, "seq", split_axis=axis_k, concat_axis=axis_k, tiled=True)
+    return block_now
 
 
 def rotate(values, positions):
@@ -79,7 +85,7 @@
         return jnp.dot(normalized_input, piece, preferred_element_type=jnp.float32)
 
     query_vectors = contract(lax.all_gather(w_query, "seq", axis=0, tiled=True))
-    key_value_pair = contract(lax.all_gather(key_value_weight, "seq", axis=0, tiled=True))
+    key_value_pair = contract(open_shelves_up(key_value_weight, 0))
     counts = token_counts[0]
     num_groups = counts.shape[0]
     starts, prefix_group, offset = layout(counts, length)

time: 542 us -> 620 us (1.14)
  local copies, waits for them, and re-layouts: 25.9 us -> 64 us
  waiting for transfers between devices: 444 us -> 469 us
  starting transfers between devices: 22 us -> 36.5 us
    all_gather x1 -> x0, waiting for transfers between devices: 149 us -> none  [shards(): lax.all_gather(key_value_weight, 'seq', axis=0, tiled=True)]
    all_to_all x0 -> x1, waiting for transfers between devices: none -> 116 us  [open_shelves_up(): lax.all_to_all(y2, 'seq', split_axis=axis_k, concat_axis=axis_k, tiled=True)]
    all_gather x1, waiting for transfers between devices: 147 us -> 245 us  [shards(): query_vectors = contract(lax.all_gather(w_query, 'seq', axis=0, tiled=True))]
    all_gather x1, waiting for transfers between devices: 44.6 us -> 0.02 us  [shards(): lax.all_gather(w_out, 'seq', axis=1, tiled=True)]
    unnamed x90 -> x147, local copies, waits for them, and re-layouts: 10.9 us -> 42.1 us
    all_to_all x0 -> x1, starting transfers between devices: none -> 19 us  [open_shelves_up(): lax.all_to_all(y2, 'seq', split_axis=axis_k, concat_axis=axis_k, tiled=True)]
    dot_general x0 -> x1, local copies, waits for them, and re-layouts: none -> 11.6 us  [contract(): return jnp.dot(normalized_input, piece, preferred_element_type=jnp.float32)]
  transfers between devices with their start and end apart: 8 -> 8, of which waited for: 8 -> 7; matrix products, arithmetic and copies ran while one was open for 9% -> 9% of each run, Pallas kernels for 0% -> 0%
where the time goes in v1:
time: 620 us; the launch traced here: 618 us
  waiting for transfers between devices  469 us (76%)
  local copies, waits for them, and re-layouts  64 us (10%)
  starting transfers between devices  36.5 us (6%)
  matrix products  23.9 us (4%)
  between operations  14.9 us (2%)
  other arithmetic  9.57 us (2%)
    all_gather x1, waiting for transfers between devices, shards(): query_vectors = contract(lax.all_gather(w_query, 'seq', axis=0, tiled=True))  245 us
    all_to_all x1, waiting for transfers between devices, open_shelves_up(): lax.all_to_all(y2, 'seq', split_axis=axis_k, concat_axis=axis_k, tiled=True)  116 us
    unnamed x147, local copies, waits for them, and re-layouts  42.1 us
    reduce_scatter x1, waiting for transfers between devices, shards(): lax.psum_scatter(partial_out.astype(jnp.bfloat16), 'tensor', scatter_dime...  30.3 us
    all_gather x1, waiting for transfers between devices, shards(): whole = lax.all_gather(hidden, 'tensor', axis=1, tiled=True)  27.8 us
    all_to_all x1, waiting for transfers between devices, shards(): lax.all_to_all(outgoing, 'seq', split_axis=0, concat_axis=0, tiled=True)  20.2 us
    all_to_all x1, starting transfers between devices, open_shelves_up(): lax.all_to_all(y2, 'seq', split_axis=axis_k, concat_axis=axis_k, tiled=True)  19 us
    all_to_all x1, waiting for transfers between devices, shards(): lax.all_to_all(out_block, 'seq', split_axis=0, concat_axis=0, tiled=True)  18.9 us
  transfers between devices with their start and end apart: 8, of which 7 were waited for; matrix products, arithmetic and copies ran while one was open for 9% of the time, Pallas kernels for 0%

profile of v1, /device:TPU:8, one launch (start us, length us, event | category | flops | bytes accessed | tf_op | source)
XLA Modules:
  0.0 618.2 jit_solution(16123494698578119703)
XLA Ops:
  7.2 1.0 constant_dynamic-update-slice_fusion.63
  8.2 0.9 constant_dynamic-update-slice_fusion.62
  9.1 0.9 constant_dynamic-update-slice_fusion.61
  10.0 0.9 constant_dynamic-update-slice_fusion.60
  10.9 0.9 constant_dynamic-update-slice_fusion.59
  11.8 0.9 constant_dynamic-update-slice_fusion.58
  12.8 0.9 constant_dynamic-update-slice_fusion.57
  13.7 0.9 constant_dynamic-update-slice_fusion.56
  14.6 0.9 constant_dynamic-update-slice_fusion.55
  16.4 0.9 constant_dynamic-update-slice_fusion.53
  19.2 0.9 constant_dynamic-update-slice_fusion.50
  21.0 0.9 constant_dynamic-update-slice_fusion.48
  21.9 0.9 constant_dynamic-update-slice_fusion.47
  23.8 0.9 constant_dynamic-update-slice_fusion.45
  26.5 0.9 constant_dynamic-update-slice_fusion.42
  28.4 0.9 constant_dynamic-update-slice_fusion.40
  29.3 0.9 constant_dynamic-update-slice_fusion.39
  31.1 0.9 constant_dynamic-update-slice_fusion.37
  33.9 0.9 constant_dynamic-update-slice_fusion.34
  37.3 3.2 copy-done.1
  40.5 19.0 %all-to-all-start.2 = ((bf16[64,64,1024]{2,1,0:T(8,128)(2,1)}), bf16[64,64,1024]{2,1,0:T(8,128)(2,1)}, u32[]{:S(2)}, u32[]{:S(2)}) async-start(bf16[64,64,1024]{2,1,0:T(8,128)(2,1)} %bitcast.158), calls=%async_computation.2 | async-start | bytes 16777216 | tf_op jit(solution)/shard_map/all_to_all | solution.py:14
  62.1 2.9 copy.123
  66.5 27.8 %all-gather.4.cloned.1.call-done = bf16[128,4096]{1,0:T(8,128)(2,1)} async-done(((bf16[128,512]{1,0:T(8,128)(2,1)}), bf16[128,4096]{1,0:T(8,128)(2,1)}) %all-gather.4.cloned.1.call-update) | async-done | bytes 1048592 | tf_op jit(solution)/shard_map/all_gather | solution.py:72
  94.3 1.5 fusion
  95.8 245.1 %all-gather.6.cloned.1.call-done = bf16[4096,512]{1,0:T(8,128)(2,1)} async-done(((bf16[64,512]{1,0:T(8,128)(2,1)}), bf16[4096,512]{1,0:T(8,128)(2,1)}) %all-gather.6.cloned.1.call-update) | async-done | bytes 4194320 | tf_op jit(solution)/shard_map/all_gather | solution.py:87
  341.0 4.3 fusion.18
  345.3 115.6 %all-to-all-done.2 = bf16[64,64,1024]{2,1,0:T(8,128)(2,1)} async-done(((bf16[64,64,1024]{2,1,0:T(8,128)(2,1)}), bf16[64,64,1024]{2,1,0:T(8,128)(2,1)}, u32[]{:S(2)}, u32[]{:S(2)}) %all-to-all-start.2) | async-done | bytes 8388640 | tf_op jit(solution)/shard_map/all_to_all | solution.py:14
  460.9 11.6 %copy.129 = bf16[1024,4096]{1,0:T(8,128)(2,1)} copy(bf16[1024,4096]{0,1:T(8,128)(2,1)} %bitcast.15) | data formatting | bytes 16777216 | tf_op jit(solution)/shard_map/dot_general | solution.py:85
  472.5 5.9 fusion.11
  478.7 1.2 gather_fusion
  480.8 5.8 all-to-all-start
  490.8 20.2 %all-to-all-done = bf16[64,4,512]{2,1,0:T(4,128)(2,1)S(1)} async-done(((bf16[64,4,512]{2,1,0:T(4,128)(2,1)}), bf16[64,4,512]{2,1,0:T(4,128)(2,1)S(1)}, u32[]{:S(2)}, u32[]{:S(2)}) %all-to-all-start) | async-done | bytes 262176 | tf_op jit(solution)/shard_map/all_to_all | solution.py:123
  511.1 1.1 fusion.69
  515.0 1.3 fusion.75
  516.3 1.0 copy-done.2
  518.7 1.4 add.237
  520.0 1.3 fusion.76
  521.3 1.0 copy-done.3
  523.7 1.4 add.235
  525.5 1.0 copy-done.5
  528.4 5.7 all-to-all-start.1
  534.2 1.2 fusion.6
  535.5 1.6 fusion.5
  539.0 9.3 %all-to-all-done.1 = bf16[64,4,4]{1,2,0:T(4,128)(2,1)S(1)} async-done(((bf16[64,4,4]{1,2,0:T(4,128)(2,1)}), bf16[64,4,4]{1,2,0:T(4,128)(2,1)S(1)}, u32[]{:S(2)}, u32[]{:S(2)}) %all-to-all-start.1) | async-done | bytes 2080 | tf_op jit(solution)/shard_map/all_to_all | solution.py:140
  548.3 5.8 all-to-all-start.3
  555.8 18.9 %all-to-all-done.3 = bf16[64,4,512]{2,1,0:T(4,128)(2,1)S(1)} async-done(((bf16[64,4,512]{2,1,0:T(4,128)(2,1)}), bf16[64,4,512]{2,1,0:T(4,128)(2,1)S(1)}, u32[]{:S(2)}, u32[]{:S(2)}) %all-to-all-start.3) | async-done | bytes 262176 | tf_op jit(solution)/shard_map/all_to_all | solution.py:139
  575.9 4.7 convolution_convert_fusion
  581.4 30.3 %reduce-scatter.2.cloned.1.call-done = bf16[128,512]{1,0:T(8,128)(2,1)} async-done(((bf16[128,4096]{1,0:T(8,128)(2,1)}), bf16[128,512]{1,0:T(8,128)(2,1)}) %reduce-scatter.2.cloned.1.call-update) | async-done | bytes 131088 | tf_op jit(solution)/shard_map/reduce_scatter | solution.py:178
  (204 shorter events, 34.9 us)
Async XLA Ops:
  7.2 29.5 %copy-start = (bf16[64,1024]{1,0:T(8,128)(2,1)S(1)}, bf16[64,1024]{1,0:T(8,128)(2,1)}, u32[]{:S(2)}) copy-start(bf16[64,1024]{1,0:T(8,128)(2,1)} %param.11) | copy-start | bytes 393220
  37.3 3.2 copy-start.1
  40.5 21.3 %copy-start.21 = (bf16[4096]{0:T(1024)(128)(2,1)S(1)}, bf16[4096]{0:T(1024)(128)(2,1)}, u32[]{:S(2)}) copy-start(bf16[4096]{0:T(1024)(128)(2,1)} %param.9) | copy-start | bytes 24580
  40.5 21.3 %copy-start.26 = (s32[1,64]{1,0:T(1,128)S(1)}, s32[1,64]{1,0:T(1,128)}, u32[]{:S(2)}) copy-start(s32[1,64]{1,0:T(1,128)} %param.15) | copy-start | bytes 772
  40.5 24.5 %copy-start.40 = (s32[64]{0:T(128)S(1)}, s32[64]{0:T(128)}, u32[]{:S(2)}) copy-start(s32[64]{0:T(128)} %param.14) | copy-start | bytes 772
  40.5 420.4 %all-to-all-start.2 = ((bf16[64,64,1024]{2,1,0:T(8,128)(2,1)}), bf16[64,64,1024]{2,1,0:T(8,128)(2,1)}, u32[]{:S(2)}, u32[]{:S(2)}) async-start(bf16[64,64,1024]{2,1,0:T(8,128)(2,1)} %bitcast.158), calls=%async_computation.2 | async-start | bytes 16777216 | tf_op jit(solution)/shard_map/all_to_all | solution.py:14
  59.5 34.8 %all-gather.4.cloned.1.call-start = ((), (), s32[]{:S(2)}) async-start(), calls=%async_computation.5 | async-start | bytes 1179648 | tf_op jit(solution)/shard_map/all_gather | solution.py:72
  60.3 280.7 %all-gather.6.cloned.1.call-start = ((), (), s32[]{:S(2)}) async-start(), calls=%async_computation.6 | async-start | bytes 4259840 | tf_op jit(solution)/shard_map/all_gather | solution.py:87
  61.0 514.9 %all-gather.8.cloned.1.call-start = ((), (), s32[]{:S(2)}) async-start(), calls=%async_computation.7 | async-start | bytes 4259840 | tf_op jit(solution)/shard_map/all_gather | solution.py:175
  460.9 11.6 %copy-start.7 = (bf16[128,4096]{1,0:T(8,128)(2,1)S(1)}, bf16[128,4096]{1,0:T(8,128)(2,1)}, u32[]{:S(2)}) copy-start(bf16[128,4096]{1,0:T(8,128)(2,1)} %all-gather.4.cloned.1.call-done) | copy-start | bytes 3145732
  480.8 30.2 %all-to-all-start = ((bf16[64,4,512]{2,1,0:T(4,128)(2,1)}), bf16[64,4,512]{2,1,0:T(4,128)(2,1)S(1)}, u32[]{:S(2)}, u32[]{:S(2)}) async-start(bf16[64,4,512]{2,1,0:T(4,128)(2,1)} %broadcast_select_fusion), calls=%async_computation | async-start | bytes 524288 | tf_op jit(solution)/shard_map/all_to_all | solution.py:123
  486.9 3.9 copy-start.27
  487.1 0.8 copy-start.29
  487.1 25.0 %copy-start.8 = (f32[128,128]{0,1:T(8,128)}, f32[128,128]{0,1:T(8,128)S(1)}, u32[]{:S(2)}) copy-start(f32[128,128]{0,1:T(8,128)S(1)} %get-tuple-element.24) | copy-start | bytes 196612
  487.2 3.6 copy-start.31
  487.9 0.6 copy-start.33
  487.9 24.2 %copy-start.10 = (f32[128,128]{0,1:T(8,128)}, f32[128,128]{0,1:T(8,128)S(1)}, u32[]{:S(2)}) copy-start(f32[128,128]{0,1:T(8,128)S(1)} %get-tuple-element.26) | copy-start | bytes 196612
  489.3 1.4 copy-start.12
  489.4 1.4 copy-start.37
  512.5 0.6 copy-start.15
  513.1 0.6 copy-start.22
  516.2 1.0 copy-start.2
  516.2 1.3 copy-start.16
  517.6 0.6 copy-start.23
  521.3 1.0 copy-start.3
  521.3 1.3 copy-start.17
  525.5 1.0 copy-start.5
  525.5 1.3 copy-start.19
  525.5 11.6 %copy-start.18 = (f32[256]{0:T(256)S(1)}, f32[256]{0:T(256)}, u32[]{:S(2)}) copy-start(f32[256]{0:T(256)} %copy-done.17) | copy-start | bytes 3076
  525.5 11.6 %copy-start.25 = (f32[256]{0:T(256)S(1)}, f32[256]{0:T(256)}, u32[]{:S(2)}) copy-start(f32[256]{0:T(256)} %copy-done.24) | copy-start | bytes 3076
  526.8 10.7 %copy-start.20 = (f32[256]{0:T(256)S(1)}, f32[256]{0:T(256)}, u32[]{:S(2)}) copy-start(f32[256]{0:T(256)} %copy-done.19) | copy-start | bytes 3076
  528.4 19.9 %all-to-all-start.1 = ((bf16[64,4,4]{1,2,0:T(4,128)(2,1)}), bf16[64,4,4]{1,2,0:T(4,128)(2,1)S(1)}, u32[]{:S(2)}, u32[]{:S(2)}) async-start(bf16[64,4,4]{1,2,0:T(4,128)(2,1)} %copy.125), calls=%async_computation.1 | async-start | bytes 131072 | tf_op jit(solution)/shard_map/all_to_all | solution.py:140
  534.1 3.0 copy-start.4
  534.1 3.4 copy-start.6
  535.4 18.8 %copy-start.9 = (f32[128,128]{0,1:T(8,128)S(1)}, f32[128,128]{0,1:T(8,128)}, u32[]{:S(2)}) copy-start(f32[128,128]{0,1:T(8,128)} %copy-done.8) | copy-start | bytes 196612
  535.4 18.8 %copy-start.30 = (f32[128]{0:T(128)S(1)}, f32[128]{0:T(128)}, u32[]{:S(2)}) copy-start(f32[128]{0:T(128)} %copy-done.29) | copy-start | bytes 1540
  535.4 18.8 %copy-start.35 = (f32[128]{0:T(128)S(1)}, f32[128]{0:T(128)}, u32[]{:S(2)}) copy-start(f32[128]{0:T(128)} %fusion.34) | copy-start | bytes 1540
  535.4 18.9 %copy-start.11 = (f32[128,128]{0,1:T(8,128)S(1)}, f32[128,128]{0,1:T(8,128)}, u32[]{:S(2)}) copy-start(f32[128,128]{0,1:T(8,128)} %copy-done.10) | copy-start | bytes 196612
  535.4 18.9 %copy-start.34 = (f32[128]{0:T(128)S(1)}, f32[128]{0:T(128)}, u32[]{:S(2)}) copy-start(f32[128]{0:T(128)} %copy-done.33) | copy-start | bytes 1540
  535.4 18.9 %copy-start.36 = (f32[128]{0:T(128)S(1)}, f32[128]{0:T(128)}, u32[]{:S(2)}) copy-start(f32[128]{0:T(128)} %fusion.33) | copy-start | bytes 1540
  535.4 19.1 %copy-start.13 = (f32[128,128]{0,1:T(8,128)S(1)}, f32[128,128]{0,1:T(8,128)}, u32[]{:S(2)}) copy-start(f32[128,128]{0,1:T(8,128)} %copy-done.12) | copy-start | bytes 196612
  535.4 19.1 %copy-start.38 = (f32[128]{0:T(128)S(1)}, f32[128]{0:T(128)}, u32[]{:S(2)}) copy-start(f32[128]{0:T(128)} %copy-done.37) | copy-start | bytes 1540
  535.4 19.1 %copy-start.39 = (f32[128]{0:T(128)S(1)}, f32[128]{0:T(128)}, u32[]{:S(2)}) copy-start(f32[128]{0:T(128)} %fusion.32) | copy-start | bytes 1540
  535.4 19.2 %copy-start.28 = (f32[128]{0:T(128)S(1)}, f32[128]{0:T(128)}, u32[]{:S(2)}) copy-start(f32[128]{0:T(128)} %copy-done.27) | copy-start | bytes 1540
  535.5 19.2 %copy-start.32 = (f32[128]{0:T(128)S(1)}, f32[128]{0:T(128)}, u32[]{:S(2)}) copy-start(f32[128]{0:T(128)} %copy-done.31) | copy-start | bytes 1540
  535.5 40.4 %copy-start.14 = (f32[128,1,128]{0,2,1:T(8,128)S(1)}, f32[128,1,128]{0,2,1:T(8,128)}, u32[]{:S(2)}) copy-start(f32[128,1,128]{0,2,1:T(8,128)} %convolution_bitcast_fusion) | copy-start | bytes 196612
  548.3 26.4 %all-to-all-start.3 = ((bf16[64,4,512]{2,1,0:T(4,128)(2,1)}), bf16[64,4,512]{2,1,0:T(4,128)(2,1)S(1)}, u32[]{:S(2)}, u32[]{:S(2)}) async-start(bf16[64,4,512]{2,1,0:T(4,128)(2,1)} %convert_element_type.83), calls=%async_computation.3 | async-start | bytes 524288 | tf_op jit(solution)/shard_map/all_to_all | solution.py:139
  554.1 57.6 %reduce-scatter.2.cloned.1.call-start = ((), (), s32[]{:S(2)}) async-start(), calls=%async_computation.8 | async-start | bytes 1179648 | tf_op jit(solution)/shard_map/reduce_scatter | solution.py:178
  (1 other events, 0.5 us)
Sparse Core Ops, SparseCore 0:
  62.5 31.7 all-gather.3
  97.2 243.6 all-gather.5
  343.9 188.8 all-gather.7
  580.7 30.8 reduce-scatter.1
